TPU v7x, 128 devices: a whole 4x4x4 slice. The times are simulated.
128 devices in a mesh: dp: 4 (over y_hi, core), head: 4 (over x), ctx: 8 (over z, y_lo).
Axes of the slice: x: 4, y: 4 (y_hi: 2, y_lo: 2; y = y_hi * 2 + y_lo), z: 4, core: 2. Of those that a mesh axis runs over, the one named last changes fastest.
Arguments:
- video: bfloat16 [16, 64, 24576], P('dp', 'head', 'ctx'), parts along dimension 0, may hold values from -6 to 6
- cache: bfloat16 [8, 64, 24576], P('dp', 'head', 'ctx'), parts along dimension 0, may hold values from -6 to 6
- conv_weight: bfloat16 [3, 3, 288, 192], replicated, may hold values from -0.125 to 0.125
- conv_bias: float32 [192], replicated, may hold values from -3 to 3
- down_weight: bfloat16 [768, 192], replicated, may hold values from -0.21875 to 0.21875
- patch_weight: bfloat16 [768, 5120], P(None, ('head', 'ctx')), may hold values from -0.21875 to 0.21875
- step_index: int32 [4], P('dp'), parts along dimension 0, may hold values from 0 to 999
- mod_weight: bfloat16 [256, 10240], P(None, ('head', 'ctx')), may hold values from -1 to 1
- qkv_weight: bfloat16 [5120, 20, 3, 128], P('ctx', 'head'), may hold values from -0.078125 to 0.078125
Outputs:
- attended: bfloat16 [16384, 2560], P(('dp', 'ctx'), 'head'), parts along dimension 0
There are 4 independent parts, one for each index of `dp`. A program takes and returns all parts, laid end to end along the dimension named above; an argument that names none is the same for every part. Nothing has to cross between parts.
All inputs are finite; a program needn't handle non-finite values.
Results may differ from a plain program's by a relative error of at most 0.015.
The roundings to bfloat16 on the way count: a program that leaves them out, or rounds other values in their place, can miss the bound.
Values may be sent and summed in bfloat16 or wider, within the bound.
No kernel may reach another device: no remote copies, remote signals or barrier semaphores. Data moves between devices by JAX's collectives and lax.ppermute only.
A program may use at most 128 MiB of HBM per device.

v0:
```python
import jax
import jax.numpy as jnp
from jax import lax
from jax.sharding import PartitionSpec as P

D = 5120
HDIM = 128
FREQ = 256


def with_halo(cells, sides, width):
    for axis, dim in sides:
        count = lax.axis_size(axis)
        ends = count - 1
        head = lax.slice_in_dim(cells, 0, width, axis=dim)
        tail = lax.slice_in_dim(cells, cells.shape[dim] - width, cells.shape[dim], axis=dim)
        cells = jnp.concatenate(
            [
                lax.ppermute(tail, axis, [(i, (i + 1) % count) for i in range(ends)]),
                cells,
                lax.ppermute(head, axis, [((i + 1) % count, i) for i in range(ends)]),
            ],
            axis=dim,
        )
    return cells


def silu_act(value):
    return value * jax.nn.sigmoid(value)


def shards(
    video,
    cache,
    conv_weight,
    conv_bias,
    down_weight,
    patch_weight,
    step_index,
    mod_weight,
    qkv_weight,
):
    cin = conv_weight.shape[2] // 3
    cmid = conv_weight.shape[3]
    frame_count = video.shape[0]
    tile_rows = video.shape[1]
    tile_cols = video.shape[2] // cin
    frames = jnp.concatenate([cache, video], 0).reshape(frame_count + 2, tile_rows, tile_cols, cin)
    padded = with_halo(frames, (("head", 1), ("ctx", 2)), 1)
    total = jnp.zeros((frame_count, tile_rows, tile_cols, cmid), jnp.float32)
    for time_tap in range(3):
        for row_tap in range(3):
            slab = padded[time_tap : time_tap + frame_count, row_tap : row_tap + tile_rows]
            stacked = jnp.concatenate(
                [slab[:, :, col_tap : col_tap + tile_cols] for col_tap in range(3)], -1
            )
            total = total + jnp.einsum(
                "fyxc,cd->fyxd",
                stacked,
                conv_weight[time_tap, row_tap],
                preferred_element_type=jnp.float32,
            )
    hidden = silu_act(total + conv_bias).astype(jnp.bfloat16)
    stacked = (
        hidden.reshape(frame_count, tile_rows // 2, 2, tile_cols // 2, 2, cmid)
        .transpose(0, 1, 3, 2, 4, 5)
        .reshape(-1, 4 * cmid)
    )
    reduced = silu_act(jnp.dot(stacked, down_weight, preferred_element_type=jnp.float32)).astype(
        jnp.bfloat16
    )
    reduced = reduced.reshape(frame_count, tile_rows // 2, tile_cols // 2, cmid)
    patches = reduced.reshape(frame_count, tile_rows // 4, 2, tile_cols // 4, 2, cmid).transpose(
        0, 1, 3, 2, 4, 5
    )
    patches = patches.reshape(-1, 4 * cmid)
    half = FREQ // 2
    freqs = jnp.exp(-jnp.log(10000.0) * jnp.arange(half, dtype=jnp.float32) / half)
    angles = step_index[0].astype(jnp.float32) * freqs
    timing = jnp.concatenate([jnp.cos(angles), jnp.sin(angles)]).astype(jnp.bfloat16)
    mod_share = jnp.dot(timing[None, :], mod_weight, preferred_element_type=jnp.float32)[0]
    modulation = lax.all_gather(
        lax.all_gather(mod_share, "ctx", axis=0, tiled=True), "head", axis=0, tiled=True
    )
    n_head = lax.axis_size("head")
    n_ctx = lax.axis_size("ctx")
    h_idx = lax.axis_index("head")
    c_idx = lax.axis_index("ctx")
    quarter = D // n_head
    scale = lax.dynamic_slice_in_dim(modulation, h_idx * quarter, quarter)
    shift = lax.dynamic_slice_in_dim(modulation, D + h_idx * quarter, quarter)
    weight_quarter = lax.all_gather(patch_weight, "ctx", axis=1, tiled=True)
    block_patches = lax.all_gather(patches, "head", axis=0, tiled=True)
    embedded = jnp.dot(block_patches, weight_quarter, preferred_element_type=jnp.float32)
    squares = lax.all_gather(jnp.sum(embedded * embedded, -1), "head", axis=0, tiled=False)
    inverse = lax.rsqrt(jnp.sum(squares, 0) / D + 1e-06)[:, None]
    normed_quarter = (embedded * inverse * (1.0 + scale) + shift).astype(jnp.bfloat16)
    normed = lax.all_gather(normed_quarter, "head", axis=1, tiled=True)
    group_rows = normed.shape[0]
    heads_here = qkv_weight.shape[1]
    out_cols = heads_here * 3 * HDIM
    local = qkv_weight.reshape(qkv_weight.shape[0], out_cols)
    rows = local.shape[0]
    half_rows = rows // 2
    core = lax.axis_index("dp") % 2
    mine = lax.dynamic_slice_in_dim(local, core * half_rows, half_rows, 0)
    fetched = jnp.stack(
        [
            lax.ppermute(mine, "ctx", [(i, (i + s) % n_ctx) for i in range(n_ctx)])
            for s in range(1, n_ctx)
        ]
    )
    n_dp = lax.axis_size("dp")
    partner = lax.ppermute(fetched, "dp", [(i, i ^ 1) for i in range(n_dp)])
    weight = jnp.concatenate(
        [local, fetched.reshape(-1, out_cols), partner.reshape(-1, out_cols)], 0
    )
    pieces = [lax.dynamic_slice_in_dim(normed, c_idx * rows, rows, 1)]
    for side in (core, 1 - core):
        for s in range(1, n_ctx):
            block = (c_idx + n_ctx - s) % n_ctx
            pieces.append(
                lax.dynamic_slice_in_dim(normed, block * rows + side * half_rows, half_rows, 1)
            )
    qkv = jnp.dot(jnp.concatenate(pieces, 1), weight, preferred_element_type=jnp.float32)
    qkv = qkv.astype(jnp.bfloat16).reshape(group_rows, heads_here, 3, HDIM)
    query = qkv[:, :, 0]
    keys = qkv[:, :, 1]
    values = qkv[:, :, 2]
    inv_root = 1.0 / jnp.sqrt(jnp.float32(HDIM))
    best = jnp.full((heads_here, group_rows), -1e30, jnp.float32)
    key_piece = lax.all_gather(keys, "ctx", axis=0, tiled=True)
    value_piece = lax.all_gather(values, "ctx", axis=0, tiled=True)
    scores = (
        jnp.einsum("qhd,khd->hqk", query, key_piece, preferred_element_type=jnp.float32) * inv_root
    )
    new_best = jnp.maximum(best, jnp.max(scores, -1))
    probs = jnp.exp(scores - new_best[..., None])
    denom = jnp.sum(probs, -1)
    accum = jnp.einsum(
        "hqk,khd->hqd", probs.astype(jnp.bfloat16), value_piece, preferred_element_type=jnp.float32
    )
    best, denom, accum = (new_best, denom, accum)
    result = (accum / denom[..., None]).astype(jnp.bfloat16)
    return result.transpose(1, 0, 2).reshape(group_rows, heads_here * HDIM)


def solution(mesh):
    return jax.shard_map(
        shards,
        mesh=mesh,
        in_specs=(
            P("dp", "head", "ctx"),
            P("dp", "head", "ctx"),
            P(),
            P(),
            P(),
            P(None, ("head", "ctx")),
            P("dp"),
            P(None, ("head", "ctx")),
            P("ctx", "head", None, None),
        ),
        out_specs=P(("dp", "ctx"), "head"),
        check_vma=False,
    )
```

profile of v0, /device:TPU:1, one launch (start us, length us, event | category | flops | bytes accessed | tf_op | source)
XLA Modules:
  0.0 616.5 jit_solution(10998383300142862645)
XLA Ops:
  6.5 3.9 copy.39
  26.3 3.7 collective-permute-start
  34.5 89.0 %all-reduce = f32[2560]{0:T(1024)} all-reduce(f32[2560]{0:T(1024)S(1)} %dynamic-update-slice), channel_id=1, replica_groups=mesh['dp'=4,'head'=4,'ctx'=8] {'ctx'}, use_global_device_ids=true, to_apply=%add | all-reduce | flops 2560 | bytes 20480
  124.2 10.9 %all-gather.4 = f32[4,1,2560]{2,1,0:T(1,128)} all-gather(f32[1,1,2560]{2,1,0:T(1,128)S(1)} %reshape.69), channel_id=1, replica_groups=mesh['dp'=4,'head'=4,'ctx'=8] {'head'}, dimensions={0}, use_global_device_ids=true | all-gather | bytes 51200 | tf_op jit(solution)/shard_map/all_gather | solution.py:82
  155.8 3.2 collective-permute-start.8
  168.7 3.4 multiply_convert_fusion
  174.5 3.1 copy.66
  177.6 3.6 reshape.54
  184.7 10.6 %all_gather.27 = bf16[512,768]{1,0:T(8,128)(2,1)S(1)} all-gather(bf16[128,768]{1,0:T(8,128)(2,1)} %reshape.55), channel_id=1, replica_groups=mesh['dp'=4,'head'=4,'ctx'=8] {'head'}, dimensions={0}, use_global_device_ids=true | all-gather | bytes 983040 | tf_op jit(solution)/shard_map/all_gather | solution.py:93
  216.1 20.7 %collective-permute-start.11 = (bf16[7,320,1920]{2,1,0:T(8,128)(2,1)}, bf16[7,320,1920]{2,1,0:T(8,128)(2,1)}, u32[]{:S(2)}, u32[]{:S(2)}) collective-permute-start(bf16[7,320,1920]{2,1,0:T(8,128)(2,1)} %bitcast_dynamic-update-slice_fusion), channel_id=1, source_target_pairs={{0,32},{32,0},{64,96},{96,64},{1,33},{33,1},{65,97},{97,65},{2,34}... | collective-permute-start | bytes 25804808 | tf_op jit(solution)/shard_map/ppermute | solution.py:114
  236.8 4.2 multiply_reduce_fusion.1
  241.0 8.1 %all-gather.3 = f32[4,1,512]{2,1,0:T(1,128)S(1)} all-gather(f32[1,1,512]{2,1,0:T(1,128)S(1)} %bitcast.133), channel_id=2, replica_groups=mesh['dp'=4,'head'=4,'ctx'=8] {'head'}, dimensions={0}, use_global_device_ids=true | all-gather | bytes 10240 | tf_op jit(solution)/shard_map/all_gather | solution.py:95
  249.1 3.2 add_convert_fusion
  252.6 3.2 copy.47
  255.8 71.6 %all-gather.12.cloned.1.call-done = bf16[512,5120]{1,0:T(8,128)(2,1)} async-done(((bf16[512,1280]{1,0:T(8,128)(2,1)}), bf16[512,5120]{1,0:T(8,128)(2,1)}) %all-gather.12.cloned.1.call-update) | async-done | bytes 5242896 | tf_op jit(solution)/shard_map/all_gather | solution.py:98
  328.6 8.0 %constant_dynamic-slice_fusion.1 = (bf16[512,320]{1,0:T(8,128)(2,1)S(1)}, bf16[512,320]{1,0:T(8,128)(2,1)S(1)}, bf16[512,320]{1,0:T(8,128)(2,1)S(1)}, bf16[512,3...) fusion(bf16[512,5120]{1,0:T(8,128)(2,1)} %all-gather.12.cloned., ...), kind=kLoop, calls=%fused_computation.165 | loop fusion | bytes 9175096 | tf_op jit(solution)/shard_map/dynamic_slice | solution.py:123
  336.6 9.1 %concatenate.94 = bf16[512,5120]{1,0:T(8,128)(2,1)} concatenate(bf16[512,640]{1,0:T(8,128)(2,1)S(1)} %constant_dynamic-slice_fusion.15, bf16[512,320]{1,0:T(8,128)(2,1)} %get-tuple-element.18, bf16[512,320]{1,0:T(8,128)(2,1)} %get-tuple-element.17, bf16[512,320]{1,0:T(8,128)(2,1)} %get-tuple-element.16, bf16[512,320]{1,0:T(8,128)(2,1)} %get-tuple-element.15, ...), dimensions={1} | concatenate | bytes 10485760 | tf_op jit(solution)/shard_map/concatenate | solution.py:125
  345.7 18.2 %fusion.13 = bf16[512,1920]{1,0:T(8,128)(2,1)} fusion(bf16[512,5120]{1,0:T(8,128)(2,1)} %concatenate.94, bf16[2240,1920]{1,0:T(8,128)(2,1)} %bitcast.42, bf16[2240,1920]{1,0:T(8,128)(2,1)} %bitcast.41, bf16[640,1920]{1,0:T(8,128)(2,1)} %copy.47), kind=kOutput, calls=%fused_computation.30 | convolution fusion | flops 10126295040 | bytes 26869760 | tf_op jit(solution)/shard_map/dot_general | solution.py:125
  363.9 2.7 copy.48
  369.2 110.1 %all-gather.14.cloned.1.call-done = bf16[4096,5,1,128]{3,0,1,2:T(8,128)(2,1)} async-done(((bf16[512,5,1,128]{3,0,1,2:T(8,128)(2,1)}), bf16[4096,5,1,128]{3,0,1,2:T(8,128)(2,1)}) %all-gather.14.cloned.1.call-update) | async-done | bytes 5242896 | tf_op jit(solution)/shard_map/all_gather | solution.py:132
  479.3 19.3 %multiply_reduce_fusion = (f32[5,512]{1,0:T(8,128)S(1)}, f32[5,512,4096]{2,1,0:T(8,128)}) fusion(bf16[4096,5,1,128]{3,0,1,2:T(8,128)(2,1)} %all-gather.14.cloned.1.call-done, bf16[512,5,3,128]{0,3,2,1:T(8,128)(2,1)S(1)} %bitcast.127), kind=kOutput, calls=%fused_computation.1 | convolution fusion | flops 2705323520 | bytes 47851520 | tf_op jit(solution)/shard_map/qhd,khd->hqk/dot_general | solution.py:135
  498.6 17.4 %fusion = f32[5,512]{1,0:T(8,128)S(1)} fusion(f32[5,512,4096]{2,1,0:T(8,128)} %get-tuple-element.61, f32[5,512]{1,0:T(8,128)S(1)} %broadcast_maximum_fusion), kind=kLoop, calls=%fused_computation.2 | loop fusion | flops 31454720 | bytes 41963520 | tf_op jit(solution)/shard_map/reduce_sum | solution.py:139
  516.0 75.3 %all-gather.16.cloned.1.call-done = bf16[4096,5,1,128]{0,3,1,2:T(8,128)(2,1)} async-done(((bf16[512,5,1,128]{0,3,1,2:T(8,128)(2,1)}), bf16[4096,5,1,128]{0,3,1,2:T(8,128)(2,1)}) %all-gather.16.cloned.1.call-update) | async-done | bytes 5242896 | tf_op jit(solution)/shard_map/all_gather | solution.py:133
  591.3 17.4 %divide_convert_fusion = bf16[512,5,128]{0,2,1:T(8,128)(2,1)S(1)} fusion(bf16[4096,5,1,128]{0,3,1,2:T(8,128)(2,1)} %all-gather.16.cloned.1.call-done, f32[5,512,4096]{2,1,0:T(8,128)} %get-tuple-element.61, f32[5,512]{1,0:T(8,128)S(1)} %broadcast_maximum_fusion, f32[512,5]{0,1:T(8,128)S(1)} %bitcast.131), kind=kOutput, calls=%fused_computation.90 | convolution fusion | flops 2716467200 | bytes 47861760 | tf_op jit(solution)/shard_map/hqk,khd->hqd/dot_general | solution.py:140
  (105 shorter events, 81.3 us)
Async XLA Ops:
  6.5 174.7 %copy-start = (bf16[768,192]{0,1:T(8,128)(2,1)S(1)}, bf16[768,192]{0,1:T(8,128)(2,1)}, u32[]{:S(2)}) copy-start(bf16[768,192]{0,1:T(8,128)(2,1)} %param.13) | copy-start | bytes 884740
  6.5 230.3 %all-gather.10.cloned.1.call-start = ((), (), s32[]{:S(2)}) async-start(), calls=%async_computation | async-start | bytes 2211840 | tf_op jit(solution)/shard_map/all_gather | solution.py:92
  10.5 11.6 %copy-start.6 = (bf16[2,16,3072]{2,1,0:T(8,128)(2,1)S(1)}, bf16[2,16,3072]{2,1,0:T(8,128)(2,1)}, u32[]{:S(2)}) copy-start(bf16[2,16,3072]{2,1,0:T(8,128)(2,1)} %param.10) | copy-start | bytes 589828
  14.8 180.5 %collective-permute-start.4 = (bf16[320,1920]{1,0:T(8,128)(2,1)}, bf16[320,1920]{1,0:T(8,128)(2,1)}, u32[]{:S(2)}, u32[]{:S(2)}) collective-permute-start(bf16[320,1920]{1,0:T(8,128)(2,1)} %copy.40), channel_id=1, source_target_pairs={{0,1},{1,2},{2,3},{3,4},{4,5},{5,6},{6,7},{7,0},{8,9},{9,10},{10,1... | collective-permute-start | bytes 3686408 | tf_op jit(solution)/shard_map/ppermute | solution.py:109
  17.0 182.2 %collective-permute-start.5 = (bf16[320,1920]{1,0:T(8,128)(2,1)}, bf16[320,1920]{1,0:T(8,128)(2,1)}, u32[]{:S(2)}, u32[]{:S(2)}) collective-permute-start(bf16[320,1920]{1,0:T(8,128)(2,1)} %copy.40), channel_id=1, source_target_pairs={{0,2},{1,3},{2,4},{3,5},{4,6},{5,7},{6,0},{7,1},{8,10},{9,11},{10,... | collective-permute-start | bytes 3686408 | tf_op jit(solution)/shard_map/ppermute | solution.py:109
  18.6 183.7 %collective-permute-start.6 = (bf16[320,1920]{1,0:T(8,128)(2,1)}, bf16[320,1920]{1,0:T(8,128)(2,1)}, u32[]{:S(2)}, u32[]{:S(2)}) collective-permute-start(bf16[320,1920]{1,0:T(8,128)(2,1)} %copy.40), channel_id=1, source_target_pairs={{0,3},{1,4},{2,5},{3,6},{4,7},{5,0},{6,1},{7,2},{8,11},{9,12},{10,... | collective-permute-start | bytes 3686408 | tf_op jit(solution)/shard_map/ppermute | solution.py:109
  21.2 183.5 %collective-permute-start.7 = (bf16[320,1920]{1,0:T(8,128)(2,1)}, bf16[320,1920]{1,0:T(8,128)(2,1)}, u32[]{:S(2)}, u32[]{:S(2)}) collective-permute-start(bf16[320,1920]{1,0:T(8,128)(2,1)} %copy.40), channel_id=1, source_target_pairs={{0,4},{1,5},{2,6},{3,7},{4,0},{5,1},{6,2},{7,3},{8,12},{9,13},{10,... | collective-permute-start | bytes 3686408 | tf_op jit(solution)/shard_map/ppermute | solution.py:109
  22.1 9.7 %copy-start.9 = (u32[128]{0:T(128)S(1)}, u32[128]{0:T(128)}, u32[]{:S(2)}) copy-start(u32[128]{0:T(128)} %constant.137) | copy-start | bytes 1540
  26.3 116.6 %collective-permute-start = (bf16[6,1,32,96]{3,2,1,0:T(8,128)(2,1)}, bf16[6,1,32,96]{3,2,1,0:T(8,128)(2,1)}, u32[]{:S(2)}, u32[]{:S(2)}) collective-permute-start(bf16[6,1,32,96]{3,2,1,0:T(8,128)(2,1)} %get-tuple-element.49), channel_id=1, source_target_pairs={{0,8},{8,16},{16,24},{1,9},{9,17},{17,25},{2,10},{10,18},{18,26},{... | collective-permute-start | bytes 110600 | tf_op jit(solution)/shard_map/ppermute | solution.py:19
  30.0 297.4 %all-gather.12.cloned.1.call-start = ((), (), s32[]{:S(2)}) async-start(), calls=%async_computation.1 | async-start | bytes 6553600 | tf_op jit(solution)/shard_map/all_gather | solution.py:98
  31.0 114.0 %copy-start.2 = (bf16[6,16,32,96]{3,2,1,0:T(8,128)(2,1)S(1)}, bf16[6,16,32,96]{3,2,1,0:T(8,128)(2,1)}, u32[]{:S(2)}) copy-start(bf16[6,16,32,96]{3,2,1,0:T(8,128)(2,1)} %reshape.52) | copy-start | bytes 1769476
  142.9 5.0 collective-permute-start.1
  148.0 2.5 collective-permute-start.2
  150.6 5.2 collective-permute-start.3
  153.8 7.3 %copy-start.7 = (bf16[3,3,288,192]{3,2,1,0:T(8,128)(2,1)S(1)}, bf16[3,3,288,192]{3,2,1,0:T(8,128)(2,1)}, u32[]{:S(2)}) copy-start(bf16[3,3,288,192]{3,2,1,0:T(8,128)(2,1)} %param.11) | copy-start | bytes 2985988
  155.8 51.4 %collective-permute-start.8 = (bf16[320,1920]{1,0:T(8,128)(2,1)}, bf16[320,1920]{1,0:T(8,128)(2,1)}, u32[]{:S(2)}, u32[]{:S(2)}) collective-permute-start(bf16[320,1920]{1,0:T(8,128)(2,1)} %copy.40), channel_id=1, source_target_pairs={{0,5},{1,6},{2,7},{3,0},{4,1},{5,2},{6,3},{7,4},{8,13},{9,14},{10,... | collective-permute-start | bytes 3686408 | tf_op jit(solution)/shard_map/ppermute | solution.py:109
  164.7 1.0 copy-start.5
  165.7 1.0 copy-start.4
  195.3 15.8 %collective-permute-start.9 = (bf16[320,1920]{1,0:T(8,128)(2,1)}, bf16[320,1920]{1,0:T(8,128)(2,1)S(1)}, u32[]{:S(2)}, u32[]{:S(2)}) collective-permute-start(bf16[320,1920]{1,0:T(8,128)(2,1)} %copy.40), channel_id=1, source_target_pairs={{0,6},{1,7},{2,0},{3,1},{4,2},{5,3},{6,4},{7,5},{8,14},{9,15},{10,... | collective-permute-start | bytes 3686408 | tf_op jit(solution)/shard_map/ppermute | solution.py:109
  199.1 15.8 %collective-permute-start.10 = (bf16[320,1920]{1,0:T(8,128)(2,1)}, bf16[320,1920]{1,0:T(8,128)(2,1)S(1)}, u32[]{:S(2)}, u32[]{:S(2)}) collective-permute-start(bf16[320,1920]{1,0:T(8,128)(2,1)} %copy.40), channel_id=1, source_target_pairs={{0,7},{1,0},{2,1},{3,2},{4,3},{5,4},{6,5},{7,6},{8,15},{9,8},{10,9... | collective-permute-start | bytes 3686408 | tf_op jit(solution)/shard_map/ppermute | solution.py:109
  216.1 129.6 %collective-permute-start.11 = (bf16[7,320,1920]{2,1,0:T(8,128)(2,1)}, bf16[7,320,1920]{2,1,0:T(8,128)(2,1)}, u32[]{:S(2)}, u32[]{:S(2)}) collective-permute-start(bf16[7,320,1920]{2,1,0:T(8,128)(2,1)} %bitcast_dynamic-update-slice_fusion), channel_id=1, source_target_pairs={{0,32},{32,0},{64,96},{96,64},{1,33},{33,1},{65,97},{97,65},{2,34}... | collective-permute-start | bytes 25804808 | tf_op jit(solution)/shard_map/ppermute | solution.py:114
  252.4 226.9 %all-gather.14.cloned.1.call-start = ((), (), s32[]{:S(2)}) async-start(), calls=%async_computation.2 | async-start | bytes 5898240 | tf_op jit(solution)/shard_map/all_gather | solution.py:132
  368.6 222.7 %all-gather.16.cloned.1.call-start = ((), (), s32[]{:S(2)}) async-start(), calls=%async_computation.3 | async-start | bytes 5898240 | tf_op jit(solution)/shard_map/all_gather | solution.py:133
  591.3 18.5 %copy-start.1 = (bf16[768,192]{0,1:T(8,128)(2,1)S(1)}, bf16[768,192]{0,1:T(8,128)(2,1)}, u32[]{:S(2)}) copy-start(bf16[768,192]{0,1:T(8,128)(2,1)} %param.13) | copy-start | bytes 884740
  (2 other events, 1.9 us)
Sparse Core Ops, SparseCore 0:
  30.1 81.6 all-gather.9
  252.5 74.8 all-gather.11
  368.7 110.5 all-gather.13
  480.8 110.4 all-gather.15
where the time goes:
time: 625 us; the launch traced here: 617 us
  waiting for transfers between devices  267 us (43%)
  blocking collectives  119 us (19%)
  local copies, waits for them, and re-layouts  77.3 us (12%)
  matrix products  71.9 us (12%)
  starting transfers between devices  41 us (7%)
  other arithmetic  25.5 us (4%)
  between operations  15.2 us (2%)
    all_gather x1, waiting for transfers between devices, shards(): key_piece = lax.all_gather(keys, 'ctx', axis=0, tiled=True)  110 us
    unnamed x1, blocking collectives  89 us
    all_gather x1, waiting for transfers between devices, shards(): value_piece = lax.all_gather(values, 'ctx', axis=0, tiled=True)  75.3 us
    all_gather x1, waiting for transfers between devices, shards(): normed = lax.all_gather(normed_quarter, 'head', axis=1, tiled=True)  71.6 us
    unnamed x35, local copies, waits for them, and re-layouts  21.6 us
    ppermute x1, starting transfers between devices, shards(): partner = lax.ppermute(fetched, 'dp', [(i, i ^ 1) for i in range(n_dp)])  20.7 us
    dot_general x1, matrix products, shards(): jnp.einsum('qhd,khd->hqk', query, key_piece, preferred_element_type=jnp.f...  19.3 us
    dot_general x1, matrix products, shards(): jnp.dot(jnp.concatenate(pieces, 1), weight, preferred_element_type=jnp.fl...  18.2 us
  transfers between devices with their start and end apart: 16, of which 8 were waited for; matrix products, arithmetic and copies ran while one was open for 20% of the time, Pallas kernels for 0%

commit v1 on v0

--- a/solution.py
+++ b/solution.py
@@ -129,8 +129,11 @@
     values = qkv[:, :, 2]
     inv_root = 1.0 / jnp.sqrt(jnp.float32(HDIM))
     best = jnp.full((heads_here, group_rows), -1e30, jnp.float32)
-    key_piece = lax.all_gather(keys, "ctx", axis=0, tiled=True)
-    value_piece = lax.all_gather(values, "ctx", axis=0, tiled=True)
+    key_piece, value_piece = jnp.split(
+        lax.all_gather(jnp.concatenate([keys, values], axis=1), "ctx", axis=0, tiled=True),
+        [keys.shape[1]],
+        axis=1,
+    )
     scores = (
         jnp.einsum("qhd,khd->hqk", query, key_piece, preferred_element_type=jnp.float32) * inv_root
     )

time: 625 us -> 664 us (1.062)
  waiting for transfers between devices: 267 us -> 296 us
  blocking collectives: 119 us -> 127 us
    all_gather x2 -> x1, waiting for transfers between devices: 185 us -> 208 us  [shards(): lax.all_gather(jnp.concatenate([keys, values], axis=1), 'ctx', axis=0, ti...]
    unnamed x1, blocking collectives: 89 us -> 97.6 us
    unnamed x35 -> x36, local copies, waits for them, and re-layouts: 21.6 us -> 21.6 us
  transfers between devices with their start and end apart: 16 -> 15, of which waited for: 8 -> 6; matrix products, arithmetic and copies ran while one was open for 20% -> 13% of each run, Pallas kernels for 0% -> 0%
where the time goes in v1:
time: 664 us; the launch traced here: 655 us
  waiting for transfers between devices  296 us (45%)
  blocking collectives  127 us (19%)
  local copies, waits for them, and re-layouts  78.2 us (12%)
  matrix products  71.7 us (11%)
  starting transfers between devices  39.1 us (6%)
  other arithmetic  28 us (4%)
  between operations  15.3 us (2%)
    all_gather x1, waiting for transfers between devices, shards(): lax.all_gather(jnp.concatenate([keys, values], axis=1), 'ctx', axis=0, ti...  208 us
    unnamed x1, blocking collectives  97.6 us
    all_gather x1, waiting for transfers between devices, shards(): normed = lax.all_gather(normed_quarter, 'head', axis=1, tiled=True)  73.6 us
    unnamed x36, local copies, waits for them, and re-layouts  21.6 us
    ppermute x1, starting transfers between devices, shards(): partner = lax.ppermute(fetched, 'dp', [(i, i ^ 1) for i in range(n_dp)])  19.3 us
    dot_general x1, matrix products, shards(): jnp.einsum('qhd,khd->hqk', query, key_piece, preferred_element_type=jnp.f...  18.8 us
    dot_general x1, matrix products, shards(): jnp.dot(jnp.concatenate(pieces, 1), weight, preferred_element_type=jnp.fl...  18.1 us
    dot_general x1, matrix products, shards(): jnp.einsum('hqk,khd->hqd', probs.astype(jnp.bfloat16), value_piece, prefe...  17.8 us
  transfers between devices with their start and end apart: 15, of which 6 were waited for; matrix products, arithmetic and copies ran while one was open for 13% of the time, Pallas kernels for 0%

profile of v1, /device:TPU:1, one launch (start us, length us, event | category | flops | bytes accessed | tf_op | source)
XLA Modules:
  0.0 655.1 jit_solution(9029111414461637670)
XLA Ops:
  6.5 3.9 copy.42
  14.8 5.6 collective-permute-start.10
  26.1 3.7 collective-permute-start
  34.3 97.6 %all-reduce = f32[2560]{0:T(1024)} all-reduce(f32[2560]{0:T(1024)S(1)} %dynamic-update-slice), channel_id=1, replica_groups=mesh['dp'=4,'head'=4,'ctx'=8] {'ctx'}, use_global_device_ids=true, to_apply=%add | all-reduce | flops 2560 | bytes 20480
  132.5 10.2 %all-gather.2 = f32[4,1,2560]{2,1,0:T(1,128)} all-gather(f32[1,1,2560]{2,1,0:T(1,128)S(1)} %reshape.67), channel_id=1, replica_groups=mesh['dp'=4,'head'=4,'ctx'=8] {'head'}, dimensions={0}, use_global_device_ids=true | all-gather | bytes 51200 | tf_op jit(solution)/shard_map/all_gather | solution.py:82
  157.5 3.1 collective-permute-done.3
  175.1 3.4 multiply_convert_fusion
  180.9 3.1 copy.71
  183.9 3.2 reshape.54
  190.6 11.0 %all_gather.24 = bf16[512,768]{1,0:T(8,128)(2,1)S(1)} all-gather(bf16[128,768]{1,0:T(8,128)(2,1)} %reshape.55), channel_id=1, replica_groups=mesh['dp'=4,'head'=4,'ctx'=8] {'head'}, dimensions={0}, use_global_device_ids=true | all-gather | bytes 983040 | tf_op jit(solution)/shard_map/all_gather | solution.py:93
  212.5 6.5 collective-permute-done.7
  228.1 19.3 %collective-permute-start.11 = (bf16[7,320,1920]{2,1,0:T(8,128)(2,1)}, bf16[7,320,1920]{2,1,0:T(8,128)(2,1)}, u32[]{:S(2)}, u32[]{:S(2)}) collective-permute-start(bf16[7,320,1920]{2,1,0:T(8,128)(2,1)} %bitcast_dynamic-update-slice_fusion), channel_id=1, source_target_pairs={{0,32},{32,0},{64,96},{96,64},{1,33},{33,1},{65,97},{97,65},{2,34}... | collective-permute-start | bytes 25804808 | tf_op jit(solution)/shard_map/ppermute | solution.py:114
  247.4 4.2 multiply_reduce_fusion.1
  251.7 8.1 %all-gather.1 = f32[4,1,512]{2,1,0:T(1,128)S(1)} all-gather(f32[1,1,512]{2,1,0:T(1,128)S(1)} %bitcast.123), channel_id=2, replica_groups=mesh['dp'=4,'head'=4,'ctx'=8] {'head'}, dimensions={0}, use_global_device_ids=true | all-gather | bytes 10240 | tf_op jit(solution)/shard_map/all_gather | solution.py:95
  259.8 3.3 add_convert_fusion
  263.3 3.3 copy.50
  266.5 73.6 %all-gather.9.cloned.1.call-done = bf16[512,5120]{1,0:T(8,128)(2,1)} async-done(((bf16[512,1280]{1,0:T(8,128)(2,1)}), bf16[512,5120]{1,0:T(8,128)(2,1)}) %all-gather.9.cloned.1.call-update) | async-done | bytes 5242896 | tf_op jit(solution)/shard_map/all_gather | solution.py:98
  341.2 8.0 %constant_dynamic-slice_fusion.1 = (bf16[512,320]{1,0:T(8,128)(2,1)S(1)}, bf16[512,320]{1,0:T(8,128)(2,1)S(1)}, bf16[512,320]{1,0:T(8,128)(2,1)S(1)}, bf16[512,3...) fusion(bf16[512,5120]{1,0:T(8,128)(2,1)} %all-gather.9.cloned.1, ...), kind=kLoop, calls=%fused_computation.165 | loop fusion | bytes 9175096 | tf_op jit(solution)/shard_map/dynamic_slice | solution.py:123
  349.2 9.0 %concatenate.97 = bf16[512,5120]{1,0:T(8,128)(2,1)} concatenate(bf16[512,640]{1,0:T(8,128)(2,1)S(1)} %constant_dynamic-slice_fusion.15, bf16[512,320]{1,0:T(8,128)(2,1)} %get-tuple-element.18, bf16[512,320]{1,0:T(8,128)(2,1)} %get-tuple-element.17, bf16[512,320]{1,0:T(8,128)(2,1)} %get-tuple-element.16, bf16[512,320]{1,0:T(8,128)(2,1)} %get-tuple-element.15, ...), dimensions={1} | concatenate | bytes 10485760 | tf_op jit(solution)/shard_map/concatenate | solution.py:125
  358.3 18.1 %fusion.13 = bf16[512,1920]{1,0:T(8,128)(2,1)} fusion(bf16[512,5120]{1,0:T(8,128)(2,1)} %concatenate.97, bf16[2240,1920]{1,0:T(8,128)(2,1)} %bitcast.42, bf16[2240,1920]{1,0:T(8,128)(2,1)} %bitcast.41, bf16[640,1920]{1,0:T(8,128)(2,1)} %copy.50), kind=kOutput, calls=%fused_computation.30 | convolution fusion | flops 10126295040 | bytes 26869760 | tf_op jit(solution)/shard_map/dot_general | solution.py:125
  384.8 208.4 %all-gather.11.cloned.1.call-done = bf16[4096,10,128]{2,0,1:T(8,128)(2,1)} async-done(((bf16[512,10,128]{2,0,1:T(8,128)(2,1)}), bf16[4096,10,128]{2,0,1:T(8,128)(2,1)}) %all-gather.11.cloned.1.call-update) | async-done | bytes 10485776 | tf_op jit(solution)/shard_map/all_gather | solution.py:133
  593.2 18.8 %multiply_reduce_fusion = (f32[5,512]{1,0:T(8,128)S(1)}, f32[5,512,4096]{2,1,0:T(8,128)}) fusion(bf16[4096,10,128]{2,0,1:T(8,128)(2,1)} %all-gather.11.cloned.1.call-done, bf16[512,5,3,128]{0,3,2,1:T(8,128)(2,1)S(1)} %bitcast.115), kind=kOutput, calls=%fused_computation.1 | convolution fusion | flops 2705323520 | bytes 47851520 | tf_op jit(solution)/shard_map/qhd,khd->hqk/dot_general | solution.py:138
  611.9 17.5 %fusion = f32[5,512]{1,0:T(8,128)S(1)} fusion(f32[5,512,4096]{2,1,0:T(8,128)} %get-tuple-element.61, f32[5,512]{1,0:T(8,128)S(1)} %broadcast_maximum_fusion), kind=kLoop, calls=%fused_computation.2 | loop fusion | flops 31454720 | bytes 41963520 | tf_op jit(solution)/shard_map/reduce_sum | solution.py:142
  629.5 17.8 %divide_convert_fusion = bf16[512,5,128]{0,2,1:T(8,128)(2,1)S(1)} fusion(bf16[4096,10,128]{2,0,1:T(8,128)(2,1)} %all-gather.11.cloned.1.call-done, f32[5,512,4096]{2,1,0:T(8,128)} %get-tuple-element.61, f32[5,512]{1,0:T(8,128)S(1)} %broadcast_maximum_fusion, f32[512,5]{0,1:T(8,128)S(1)} %bitcast.122), kind=kOutput, calls=%fused_computation.91 | convolution fusion | flops 2716467200 | bytes 47861760 | tf_op jit(solution)/shard_map/hqk,khd->hqd/dot_general | solution.py:143
  (104 shorter events, 79.3 us)
Async XLA Ops:
  6.5 180.6 %copy-start = (bf16[768,192]{0,1:T(8,128)(2,1)S(1)}, bf16[768,192]{0,1:T(8,128)(2,1)}, u32[]{:S(2)}) copy-start(bf16[768,192]{0,1:T(8,128)(2,1)} %param.13) | copy-start | bytes 884740
  6.5 240.9 %all-gather.7.cloned.1.call-start = ((), (), s32[]{:S(2)}) async-start(), calls=%async_computation | async-start | bytes 2211840 | tf_op jit(solution)/shard_map/all_gather | solution.py:92
  12.2 9.7 %copy-start.6 = (bf16[2,16,3072]{2,1,0:T(8,128)(2,1)S(1)}, bf16[2,16,3072]{2,1,0:T(8,128)(2,1)}, u32[]{:S(2)}) copy-start(bf16[2,16,3072]{2,1,0:T(8,128)(2,1)} %param.10) | copy-start | bytes 589828
  14.8 210.9 %collective-permute-start.10 = (bf16[320,1920]{1,0:T(8,128)(2,1)}, bf16[320,1920]{1,0:T(8,128)(2,1)}, u32[]{:S(2)}, u32[]{:S(2)}) collective-permute-start(bf16[320,1920]{1,0:T(8,128)(2,1)} %copy.43), channel_id=1, source_target_pairs={{0,7},{1,0},{2,1},{3,2},{4,3},{5,4},{6,5},{7,6},{8,15},{9,8},{10,9... | collective-permute-start | bytes 3686408 | tf_op jit(solution)/shard_map/ppermute | solution.py:109
  20.4 202.9 %collective-permute-start.9 = (bf16[320,1920]{1,0:T(8,128)(2,1)}, bf16[320,1920]{1,0:T(8,128)(2,1)}, u32[]{:S(2)}, u32[]{:S(2)}) collective-permute-start(bf16[320,1920]{1,0:T(8,128)(2,1)} %copy.43), channel_id=1, source_target_pairs={{0,6},{1,7},{2,0},{3,1},{4,2},{5,3},{6,4},{7,5},{8,14},{9,15},{10,... | collective-permute-start | bytes 3686408 | tf_op jit(solution)/shard_map/ppermute | solution.py:109
  20.5 189.6 %collective-permute-start.6 = (bf16[320,1920]{1,0:T(8,128)(2,1)}, bf16[320,1920]{1,0:T(8,128)(2,1)}, u32[]{:S(2)}, u32[]{:S(2)}) collective-permute-start(bf16[320,1920]{1,0:T(8,128)(2,1)} %copy.43), channel_id=1, source_target_pairs={{0,3},{1,4},{2,5},{3,6},{4,7},{5,0},{6,1},{7,2},{8,11},{9,12},{10,... | collective-permute-start | bytes 3686408 | tf_op jit(solution)/shard_map/ppermute | solution.py:109
  20.5 184.8 %collective-permute-start.5 = (bf16[320,1920]{1,0:T(8,128)(2,1)}, bf16[320,1920]{1,0:T(8,128)(2,1)}, u32[]{:S(2)}, u32[]{:S(2)}) collective-permute-start(bf16[320,1920]{1,0:T(8,128)(2,1)} %copy.43), channel_id=1, source_target_pairs={{0,2},{1,3},{2,4},{3,5},{4,6},{5,7},{6,0},{7,1},{8,10},{9,11},{10,... | collective-permute-start | bytes 3686408 | tf_op jit(solution)/shard_map/ppermute | solution.py:109
  21.9 9.7 %copy-start.9 = (u32[128]{0:T(128)S(1)}, u32[128]{0:T(128)}, u32[]{:S(2)}) copy-start(u32[128]{0:T(128)} %constant.137) | copy-start | bytes 1540
  21.9 318.2 %all-gather.9.cloned.1.call-start = ((), (), s32[]{:S(2)}) async-start(), calls=%async_computation.1 | async-start | bytes 6553600 | tf_op jit(solution)/shard_map/all_gather | solution.py:98
  26.1 124.4 %collective-permute-start = (bf16[6,1,32,96]{3,2,1,0:T(8,128)(2,1)}, bf16[6,1,32,96]{3,2,1,0:T(8,128)(2,1)}, u32[]{:S(2)}, u32[]{:S(2)}) collective-permute-start(bf16[6,1,32,96]{3,2,1,0:T(8,128)(2,1)} %get-tuple-element.49), channel_id=1, source_target_pairs={{0,8},{8,16},{16,24},{1,9},{9,17},{17,25},{2,10},{10,18},{18,26},{... | collective-permute-start | bytes 110600 | tf_op jit(solution)/shard_map/ppermute | solution.py:19
  30.8 121.8 %copy-start.2 = (bf16[6,16,32,96]{3,2,1,0:T(8,128)(2,1)S(1)}, bf16[6,16,32,96]{3,2,1,0:T(8,128)(2,1)}, u32[]{:S(2)}) copy-start(bf16[6,16,32,96]{3,2,1,0:T(8,128)(2,1)} %reshape.52) | copy-start | bytes 1769476
  150.5 5.0 collective-permute-start.1
  155.7 4.9 collective-permute-start.3
  160.6 3.9 collective-permute-start.2
  164.4 3.1 copy-start.5
  164.4 3.1 copy-start.7
  164.4 37.2 %collective-permute-start.4 = (bf16[320,1920]{1,0:T(8,128)(2,1)}, bf16[320,1920]{1,0:T(8,128)(2,1)}, u32[]{:S(2)}, u32[]{:S(2)}) collective-permute-start(bf16[320,1920]{1,0:T(8,128)(2,1)} %copy.43), channel_id=1, source_target_pairs={{0,1},{1,2},{2,3},{3,4},{4,5},{5,6},{6,7},{7,0},{8,9},{9,10},{10,1... | collective-permute-start | bytes 3686408 | tf_op jit(solution)/shard_map/ppermute | solution.py:109
  170.3 1.0 copy-start.4
  173.1 1.0 copy-start.3
  201.7 17.3 %collective-permute-start.7 = (bf16[320,1920]{1,0:T(8,128)(2,1)}, bf16[320,1920]{1,0:T(8,128)(2,1)S(1)}, u32[]{:S(2)}, u32[]{:S(2)}) collective-permute-start(bf16[320,1920]{1,0:T(8,128)(2,1)} %copy.43), channel_id=1, source_target_pairs={{0,4},{1,5},{2,6},{3,7},{4,0},{5,1},{6,2},{7,3},{8,12},{9,13},{10,... | collective-permute-start | bytes 3686408 | tf_op jit(solution)/shard_map/ppermute | solution.py:109
  205.3 16.8 %collective-permute-start.8 = (bf16[320,1920]{1,0:T(8,128)(2,1)}, bf16[320,1920]{1,0:T(8,128)(2,1)S(1)}, u32[]{:S(2)}, u32[]{:S(2)}) collective-permute-start(bf16[320,1920]{1,0:T(8,128)(2,1)} %copy.43), channel_id=1, source_target_pairs={{0,5},{1,6},{2,7},{3,0},{4,1},{5,2},{6,3},{7,4},{8,13},{9,14},{10,... | collective-permute-start | bytes 3686408 | tf_op jit(solution)/shard_map/ppermute | solution.py:109
  228.1 130.1 %collective-permute-start.11 = (bf16[7,320,1920]{2,1,0:T(8,128)(2,1)}, bf16[7,320,1920]{2,1,0:T(8,128)(2,1)}, u32[]{:S(2)}, u32[]{:S(2)}) collective-permute-start(bf16[7,320,1920]{2,1,0:T(8,128)(2,1)} %bitcast_dynamic-update-slice_fusion), channel_id=1, source_target_pairs={{0,32},{32,0},{64,96},{96,64},{1,33},{33,1},{65,97},{97,65},{2,34}... | collective-permute-start | bytes 25804808 | tf_op jit(solution)/shard_map/ppermute | solution.py:114
  263.1 330.1 %all-gather.11.cloned.1.call-start = ((), (), s32[]{:S(2)}) async-start(), calls=%async_computation.2 | async-start | bytes 11796480 | tf_op jit(solution)/shard_map/all_gather | solution.py:133
  629.4 18.9 %copy-start.1 = (bf16[768,192]{0,1:T(8,128)(2,1)S(1)}, bf16[768,192]{0,1:T(8,128)(2,1)}, u32[]{:S(2)}) copy-start(bf16[768,192]{0,1:T(8,128)(2,1)} %param.13) | copy-start | bytes 884740
  (1 other events, 0.9 us)
Sparse Core Ops, SparseCore 0:
  22.0 88.8 all-gather.6
  263.2 76.8 all-gather.8
  384.9 208.1 all-gather.10
